TPU v7x, 512 devices: a whole 4x4x16 slice. The times are simulated.
512 devices in a mesh: smp: 16 (over z), par: 32 (over x, y, core).
Axes of the slice: x: 4, y: 4, z: 16, core: 2. Of those that a mesh axis runs over, the one named last changes fastest.
Arguments:
- jacobian: bfloat16 [4096, 16384], P('smp', 'par'), may hold values from -52 to 52
Outputs:
- panel_factor: float32 [4096, 512], P('smp')
- schur_part: float32 [4096, 4096], P('smp', 'par')
All inputs are finite; a program needn't handle non-finite values.
Results may differ from a plain program's by a relative error of at most 0.0022.
Values may be sent and summed in bfloat16 or wider, within the bound.
No kernel may reach another device: no remote copies, remote signals or barrier semaphores. Data moves between devices by JAX's collectives and lax.ppermute only.
A program may use at most 64 MiB of HBM per device.

v0:
```python
import jax
import jax.numpy as jnp
from jax import lax
from jax.sharding import PartitionSpec as P

PANEL = 512
shift_scale = 0.01


def shards(jacobian):
    row_count, par_width = jacobian.shape
    par_count = lax.axis_size("par")
    smp_count = lax.axis_size("smp")
    sample_total = row_count * smp_count
    param_total = par_width * par_count
    col_width = sample_total // par_count
    row_index = lax.axis_index("smp")
    col_index = lax.axis_index("par")
    widened = jacobian.astype(jnp.float32)
    col_mean = lax.psum(jnp.sum(widened, axis=0), "smp") / sample_total
    centered = (widened - col_mean).astype(jnp.bfloat16)
    gathered = lax.all_gather(centered, "smp", axis=0, tiled=True)
    gram_tile = lax.psum_scatter(
        lax.dot_general(
            gathered, centered, (((1,), (1,)), ((), ())), preferred_element_type=jnp.float32
        )
        / param_total,
        "par",
        scatter_dimension=0,
        tiled=True,
    ).T
    global_rows = row_index * row_count + jnp.arange(row_count, dtype=jnp.int32)
    global_cols = col_index * col_width + jnp.arange(col_width, dtype=jnp.int32)
    diag_mask = global_rows[:, None] == global_cols[None, :]
    trace_total = lax.psum(jnp.sum(jnp.where(diag_mask, gram_tile, 0.0)), ("smp", "par"))
    shift_value = shift_scale * trace_total / sample_total
    shifted = gram_tile + jnp.where(diag_mask, shift_value, 0.0)
    col_keep = (col_index < PANEL // col_width).astype(jnp.float32)
    start_col = jnp.minimum(col_index, PANEL // col_width - 1) * col_width
    placed_rows = lax.dynamic_update_slice(
        jnp.zeros((row_count, PANEL), jnp.float32), shifted * col_keep, (jnp.int32(0), start_col)
    )
    panel_rows = lax.psum(placed_rows, "par")
    row_keep = (row_index < PANEL // row_count).astype(jnp.float32)
    start_row = jnp.minimum(row_index, PANEL // row_count - 1) * row_count
    top_square = lax.dynamic_update_slice(
        jnp.zeros((PANEL, PANEL), jnp.float32), panel_rows * row_keep, (start_row, jnp.int32(0))
    )
    top_band = lax.dynamic_update_slice(
        jnp.zeros((PANEL, col_width), jnp.float32), shifted * row_keep, (start_row, jnp.int32(0))
    )
    square, band_rows = lax.psum((top_square, top_band), "smp")
    factor = jnp.linalg.cholesky(square)
    panel_out = jax.scipy.linalg.solve_triangular(factor, panel_rows.T, lower=True).T
    band_factor = jax.scipy.linalg.solve_triangular(factor, band_rows, lower=True)
    schur_tile = shifted - jnp.dot(panel_out, band_factor, precision=lax.Precision.HIGHEST)
    return (panel_out, schur_tile)


def solution(mesh):
    placed = (P("smp", "par"),)
    return jax.shard_map(
        shards,
        mesh=mesh,
        in_specs=placed,
        out_specs=(P("smp", None), P("smp", "par")),
        check_vma=False,
    )
```

profile of v0, /device:TPU:2, one launch (start us, length us, event | category | flops | bytes accessed | tf_op | source)
XLA Modules:
  0.0 757.3 jit_solution(15600301314958486580)
XLA Ops:
  8.2 36.5 %psum.35 = f32[512]{0:T(512)S(1)} all-reduce(f32[512]{0:T(512)S(1)} %convert_reduce_fusion), channel_id=1, replica_groups=mesh['smp'=16,'par'=32] {'smp'}, use_global_device_ids=true, to_apply=%region_1.0 | all-reduce | flops 512 | bytes 4096 | tf_op jit(solution)/shard_map/psum | solution.py:20
  44.7 1.7 fusion.1
  46.5 74.9 %all-gather.2.cloned.1.call-done = bf16[4096,512]{1,0:T(8,128)(2,1)} async-done(((bf16[256,512]{1,0:T(8,128)(2,1)}), bf16[4096,512]{1,0:T(8,128)(2,1)}) %all-gather.2.cloned.1.call-update) | async-done | bytes 4194320 | tf_op jit(solution)/shard_map/all_gather | solution.py:22
  121.4 5.4 convolution_multiply_fusion
  126.9 101.3 %reduce-scatter.2.cloned.1.call-done = f32[128,256]{1,0:T(8,128)} async-done(((f32[4096,256]{1,0:T(8,128)}), f32[128,256]{1,0:T(8,128)}) %reduce-scatter.2.cloned.1.call-update) | async-done | bytes 131088 | tf_op jit(solution)/shard_map/reduce_scatter | solution.py:23
  228.2 1.6 fusion.29
  229.8 101.8 %psum.36 = f32[]{:T(128)} all-reduce(f32[]{:T(128)} %fusion.29), channel_id=1, replica_groups=mesh['smp'=16,'par'=32] {'smp','par'}, use_global_device_ids=true, to_apply=%region_4.5 | all-reduce | flops 1 | bytes 8 | tf_op jit(solution)/shard_map/psum | solution.py:35
  334.4 130.4 %all-reduce.5.cloned.1.call-done = f32[256,512]{0,1:T(8,128)} async-done(((f32[256,512]{0,1:T(8,128)}), f32[256,512]{0,1:T(8,128)}) %all-reduce.5.cloned.1.call-update) | async-done | bytes 524304 | tf_op jit(solution)/shard_map/psum | solution.py:43
  467.1 140.6 %all-reduce.7.cloned.1.call-done = (f32[512,512]{0,1:T(8,128)}, f32[512,128]{0,1:T(8,128)}) async-done(((f32[512,512]{0,1:T(8,128)}, f32[512,128]{0,1:T(8,128)}), (f32[512,512]{0,1:T(8,128)}, f32[512,128]{0,1:T(8,128)})) %all-reduce.7.cloned.1.call-update) | async-done | bytes 1310736 | tf_op jit(solution)/shard_map/psum | solution.py:52
  607.7 1.6 copy.3
  609.3 1.4 fusion
  610.7 11.7 %cholesky.103 = f32[128,128]{1,0:T(8,128)S(1)} custom-call(f32[128,128]{1,0:T(8,128)S(1)} %cholesky.263), custom_call_target="Cholesky" | custom-call | tf_op jit(solution)/shard_map/jit(cholesky)/cholesky | solution.py:53
  622.5 9.8 %custom-call.34 = f32[1,128,128]{1,2,0:T(8,128)S(1)} custom-call(f32[1,128,128]{2,1,0:T(8,128)S(1)} %get-tuple-element.35), custom_call_target="InvertDiagBlocksLowerTriangular" | custom-call | tf_op jit(solution)/shard_map/jit(cholesky)/cholesky | solution.py:53
  633.0 11.7 %cholesky.215 = f32[128,128]{1,0:T(8,128)S(1)} custom-call(f32[128,128]{1,0:T(8,128)S(1)} %cholesky.267), custom_call_target="Cholesky" | custom-call | tf_op jit(solution)/shard_map/jit(cholesky)/cholesky | solution.py:53
  645.2 10.0 %custom-call.35 = f32[1,128,128]{1,2,0:T(8,128)S(1)} custom-call(f32[1,128,128]{2,1,0:T(8,128)S(1)} %get-tuple-element.33), custom_call_target="InvertDiagBlocksLowerTriangular" | custom-call | tf_op jit(solution)/shard_map/jit(cholesky)/cholesky | solution.py:53
  656.2 11.7 %cholesky.236 = f32[128,128]{1,0:T(8,128)S(1)} custom-call(f32[128,128]{1,0:T(8,128)S(1)} %cholesky.272), custom_call_target="Cholesky" | custom-call | tf_op jit(solution)/shard_map/jit(cholesky)/cholesky | solution.py:53
  668.0 9.8 %custom-call.36 = f32[1,128,128]{1,2,0:T(8,128)S(1)} custom-call(f32[1,128,128]{2,1,0:T(8,128)S(1)} %get-tuple-element.31), custom_call_target="InvertDiagBlocksLowerTriangular" | custom-call | tf_op jit(solution)/shard_map/jit(cholesky)/cholesky | solution.py:53
  678.6 11.9 %cholesky.253 = f32[128,128]{1,0:T(8,128)S(1)} custom-call(f32[128,128]{1,0:T(8,128)S(1)} %convolution_subtract_fusion.9), custom_call_target="Cholesky" | custom-call | tf_op jit(solution)/shard_map/jit(cholesky)/cholesky | solution.py:53
  695.4 8.8 %while.1 = (s32[]{:T(128)}, f32[512,512]{0,1:T(8,128)S(1)}, s32[4,2]{0,1:T(2,128)S(1)}, f32[4,128,128]{2,1,0:T(8,128)S(1)}, s32[]{:T(128)}) while((s32[]{:T(128)}, f32[512,512]{0,1:T(8,128)S(1)}, s32[4,2]{0,1:T(2,128)S(1)}, f32[4,128,128]{2,1,0:T(8,128)S(1)}, s32[]{:T(128)}) %tuple.30), condition=%wide.while_cond, body=%wide.while_body.sunk | while | flops 2 | bytes 393321 | solution.py:54
  696.1 1.4 dynamic-slice.7
  698.3 1.4 dynamic-slice.7
  700.5 1.4 dynamic-slice.7
  702.6 1.4 dynamic-slice.7
  704.2 39.3 %custom-call.37 = f32[4,128,128]{1,2,0:T(8,128)S(1)} custom-call(f32[4,128,128]{2,1,0:T(8,128)S(1)} %get-tuple-element.9), custom_call_target="InvertDiagBlocksLowerTriangular" | custom-call | tf_op jit(solution)/shard_map/jit(_solve_triangular)/triangular_solve | solution.py:54
  (93 shorter events, 21.0 us)
Async XLA Ops:
  7.2 114.2 %all-gather.2.cloned.1.call-start = ((), (), s32[]{:S(2)}) async-start(), calls=%async_computation.1 | async-start | bytes 4456448 | tf_op jit(solution)/shard_map/all_gather | solution.py:22
  46.5 181.7 %reduce-scatter.2.cloned.1.call-start = ((), (), s32[]{:S(2)}) async-start(), calls=%async_computation.2 | async-start | bytes 4325376 | tf_op jit(solution)/shard_map/reduce_scatter | solution.py:23
  126.8 337.9 %all-reduce.5.cloned.1.call-start = ((), (), s32[]{:S(2)}) async-start(), calls=%async_computation.3 | async-start | bytes 1048576 | tf_op jit(solution)/shard_map/psum | solution.py:43
  333.3 0.8 copy-start.2
  333.4 132.6 %copy-start.3 = (f32[512,128]{0,1:T(8,128)}, f32[512,128]{0,1:T(8,128)S(1)}, u32[]{:S(2)}) copy-start(f32[512,128]{0,1:T(8,128)S(1)} %get-tuple-element.28) | copy-start | bytes 786436
  334.2 273.6 %all-reduce.7.cloned.1.call-start = ((), (), s32[]{:S(2)}) async-start(), calls=%async_computation.4 | async-start | bytes 2621440 | tf_op jit(solution)/shard_map/psum | solution.py:52
  466.0 1.0 copy-start
  645.0 98.5 %copy-start.5 = (f32[512,128]{0,1:T(8,128)S(1)}, f32[512,128]{0,1:T(8,128)}, u32[]{:S(2)}) copy-start(f32[512,128]{0,1:T(8,128)} %get-tuple-element.25) | copy-start | bytes 786436
  655.6 90.3 %copy-start.1 = (f32[256,512]{0,1:T(8,128)S(1)}, f32[256,512]{0,1:T(8,128)}, u32[]{:S(2)}) copy-start(f32[256,512]{0,1:T(8,128)} %all-reduce.5.cloned.1.call-done) | copy-start | bytes 1572868
  695.4 53.0 %copy-start.4 = (f32[128,256]{1,0:T(8,128)S(1)}, f32[128,256]{1,0:T(8,128)}, u32[]{:S(2)}) copy-start(f32[128,256]{1,0:T(8,128)} %reduce-scatter.2.cloned.1.call-done) | copy-start | bytes 393220
Sparse Core Ops, SparseCore 0:
  46.6 74.7 all-gather.1
  126.9 101.1 reduce-scatter.1
  334.3 130.4 all-reduce.4
  467.2 140.4 all-reduce.6
where the time goes:
time: 758 us; the launch traced here: 757 us
  waiting for transfers between devices  447 us (59%)
  blocking collectives  138 us (18%)
  other arithmetic  126 us (17%)
  between operations  17.4 us (2%)
  local copies, waits for them, and re-layouts  14.6 us (2%)
  matrix products  13.1 us (2%)
    psum x1, waiting for transfers between devices, shards(): square, band_rows = lax.psum((top_square, top_band), 'smp')  141 us
    psum x1, waiting for transfers between devices, shards(): panel_rows = lax.psum(placed_rows, 'par')  130 us
    psum x1, blocking collectives, shards(): lax.psum(jnp.sum(jnp.where(diag_mask, gram_tile, 0.0)), ('smp', 'par'))  102 us
    reduce_scatter x1, waiting for transfers between devices, shards(): lax.psum_scatter(lax.dot_general(gathered, centered, (((1,), (1,)), ((),...  101 us
    another operation x14, other arithmetic, shards(): factor = jnp.linalg.cholesky(square)  78.8 us
    all_gather x1, waiting for transfers between devices, shards(): gathered = lax.all_gather(centered, 'smp', axis=0, tiled=True)  74.9 us
    another operation x3, other arithmetic, shards(): jax.scipy.linalg.solve_triangular(factor, panel_rows.T, lower=True)  39.4 us
    psum x1, blocking collectives, shards(): col_mean = lax.psum(jnp.sum(widened, axis=0), 'smp') / sample_total  36.5 us
  transfers between devices with their start and end apart: 4, of which 4 were waited for; matrix products, arithmetic and copies ran while one was open for 0% of the time, Pallas kernels for 0%

commit v1 on v0

--- a/solution.py
+++ b/solution.py
@@ -2,6 +2,7 @@
 import jax.numpy as jnp
 from jax import lax
 from jax.sharding import PartitionSpec as P
+from jax.lax import all_to_all, psum
 
 PANEL = 512
 shift_scale = 0.01
@@ -19,7 +20,9 @@
     widened = jacobian.astype(jnp.float32)
     col_mean = lax.psum(jnp.sum(widened, axis=0), "smp") / sample_total
     centered = (widened - col_mean).astype(jnp.bfloat16)
-    gathered = lax.all_gather(centered, "smp", axis=0, tiled=True)
+    num = psum(1, "smp")
+    slots = [num if s == 0 else 1 for s in range(centered.ndim)]
+    gathered = all_to_all(jnp.tile(centered, slots), "smp", concat_axis=0, split_axis=0, tiled=True)
     gram_tile = lax.psum_scatter(
         lax.dot_general(
             gathered, centered, (((1,), (1,)), ((), ())), preferred_element_type=jnp.float32

time: 758 us -> 865 us (1.14)
  blocking collectives: 138 us -> 324 us
  waiting for transfers between devices: 447 us -> 372 us
    all_to_all x0 -> x1, blocking collectives: none -> 185 us  [shards(): all_to_all(jnp.tile(centered, slots), 'smp', concat_axis=0, split_axis=0,...]
    all_gather x1 -> x0, waiting for transfers between devices: 74.9 us -> none  [shards(): gathered = lax.all_gather(centered, 'smp', axis=0, tiled=True)]
  transfers between devices with their start and end apart: 4 -> 3, of which waited for: 4 -> 3; matrix products, arithmetic and copies ran while one was open for 0% -> 0% of each run, Pallas kernels for 0% -> 0%
where the time goes in v1:
time: 865 us
  waiting for transfers between devices  372 us (43%)
  blocking collectives  324 us (37%)
  other arithmetic  126 us (15%)
  between operations  17.4 us (2%)
  local copies, waits for them, and re-layouts  15 us (2%)
  matrix products  10.9 us (1%)
    all_to_all x1, blocking collectives, shards(): all_to_all(jnp.tile(centered, slots), 'smp', concat_axis=0, split_axis=0,...  185 us
    psum x1, waiting for transfers between devices, shards(): square, band_rows = lax.psum((top_square, top_band), 'smp')  141 us
    psum x1, waiting for transfers between devices, shards(): panel_rows = lax.psum(placed_rows, 'par')  130 us
    psum x1, blocking collectives, shards(): lax.psum(jnp.sum(jnp.where(diag_mask, gram_tile, 0.0)), ('smp', 'par'))  102 us
    reduce_scatter x1, waiting for transfers between devices, shards(): lax.psum_scatter(lax.dot_general(gathered, centered, (((1,), (1,)), ((),...  101 us
    another operation x14, other arithmetic, shards(): factor = jnp.linalg.cholesky(square)  78.8 us
    another operation x3, other arithmetic, shards(): jax.scipy.linalg.solve_triangular(factor, panel_rows.T, lower=True)  39.4 us
    psum x1, blocking collectives, shards(): col_mean = lax.psum(jnp.sum(widened, axis=0), 'smp') / sample_total  36.5 us
  transfers between devices with their start and end apart: 3, of which 3 were waited for; matrix products, arithmetic and copies ran while one was open for 0% of the time, Pallas kernels for 0%

profile of v1, /device:TPU:2, one launch (start us, length us, event | category | flops | bytes accessed | tf_op | source)
XLA Modules:
  0.0 864.8 jit_solution(3920713979308305435)
XLA Ops:
  8.2 36.5 %psum.35 = f32[512]{0:T(512)S(1)} all-reduce(f32[512]{0:T(512)S(1)} %convert_reduce_fusion), channel_id=1, replica_groups=mesh['smp'=16,'par'=32] {'smp'}, use_global_device_ids=true, to_apply=%region_1.0 | all-reduce | flops 512 | bytes 4096 | tf_op jit(solution)/shard_map/psum | solution.py:21
  46.1 185.3 %all_to_all.9 = bf16[16,256,512]{2,1,0:T(8,128)(2,1)S(1)} all-to-all(bf16[16,256,512]{2,1,0:T(8,128)(2,1)S(1)} %tile.2), channel_id=1, replica_groups=mesh['smp'=16,'par'=32] {'smp'}, dimensions={0} | all-to-all | bytes 8388608 | tf_op jit(solution)/shard_map/all_to_all | solution.py:25
  231.4 3.2 convolution_multiply_fusion
  234.8 100.9 %reduce-scatter.2.cloned.1.call-done = f32[128,256]{1,0:T(8,128)} async-done(((f32[4096,256]{1,0:T(8,128)}), f32[128,256]{1,0:T(8,128)}) %reduce-scatter.2.cloned.1.call-update) | async-done | bytes 131088 | tf_op jit(solution)/shard_map/reduce_scatter | solution.py:26
  335.7 1.6 fusion.29
  337.3 101.8 %psum.36 = f32[]{:T(128)} all-reduce(f32[]{:T(128)} %fusion.29), channel_id=1, replica_groups=mesh['smp'=16,'par'=32] {'smp','par'}, use_global_device_ids=true, to_apply=%region_4.5 | all-reduce | flops 1 | bytes 8 | tf_op jit(solution)/shard_map/psum | solution.py:38
  441.9 130.3 %all-reduce.5.cloned.1.call-done = f32[256,512]{0,1:T(8,128)} async-done(((f32[256,512]{0,1:T(8,128)}), f32[256,512]{0,1:T(8,128)}) %all-reduce.5.cloned.1.call-update) | async-done | bytes 524304 | tf_op jit(solution)/shard_map/psum | solution.py:46
  572.4 1.1 multiply_dynamic-update-slice_fusion
  574.6 140.7 %all-reduce.7.cloned.1.call-done = (f32[512,512]{0,1:T(8,128)}, f32[512,128]{0,1:T(8,128)}) async-done(((f32[512,512]{0,1:T(8,128)}, f32[512,128]{0,1:T(8,128)}), (f32[512,512]{0,1:T(8,128)}, f32[512,128]{0,1:T(8,128)})) %all-reduce.7.cloned.1.call-update) | async-done | bytes 1310736 | tf_op jit(solution)/shard_map/psum | solution.py:55
  715.2 1.6 copy.3
  716.8 1.4 fusion
  718.3 11.7 %cholesky.103 = f32[128,128]{1,0:T(8,128)S(1)} custom-call(f32[128,128]{1,0:T(8,128)S(1)} %cholesky.263), custom_call_target="Cholesky" | custom-call | tf_op jit(solution)/shard_map/jit(cholesky)/cholesky | solution.py:56
  730.0 9.8 %custom-call.34 = f32[1,128,128]{1,2,0:T(8,128)S(1)} custom-call(f32[1,128,128]{2,1,0:T(8,128)S(1)} %get-tuple-element.35), custom_call_target="InvertDiagBlocksLowerTriangular" | custom-call | tf_op jit(solution)/shard_map/jit(cholesky)/cholesky | solution.py:56
  740.5 11.7 %cholesky.215 = f32[128,128]{1,0:T(8,128)S(1)} custom-call(f32[128,128]{1,0:T(8,128)S(1)} %cholesky.267), custom_call_target="Cholesky" | custom-call | tf_op jit(solution)/shard_map/jit(cholesky)/cholesky | solution.py:56
  752.7 10.0 %custom-call.35 = f32[1,128,128]{1,2,0:T(8,128)S(1)} custom-call(f32[1,128,128]{2,1,0:T(8,128)S(1)} %get-tuple-element.33), custom_call_target="InvertDiagBlocksLowerTriangular" | custom-call | tf_op jit(solution)/shard_map/jit(cholesky)/cholesky | solution.py:56
  763.7 11.7 %cholesky.236 = f32[128,128]{1,0:T(8,128)S(1)} custom-call(f32[128,128]{1,0:T(8,128)S(1)} %cholesky.272), custom_call_target="Cholesky" | custom-call | tf_op jit(solution)/shard_map/jit(cholesky)/cholesky | solution.py:56
  775.6 9.8 %custom-call.36 = f32[1,128,128]{1,2,0:T(8,128)S(1)} custom-call(f32[1,128,128]{2,1,0:T(8,128)S(1)} %get-tuple-element.31), custom_call_target="InvertDiagBlocksLowerTriangular" | custom-call | tf_op jit(solution)/shard_map/jit(cholesky)/cholesky | solution.py:56
  786.2 11.9 %cholesky.253 = f32[128,128]{1,0:T(8,128)S(1)} custom-call(f32[128,128]{1,0:T(8,128)S(1)} %convolution_subtract_fusion.9), custom_call_target="Cholesky" | custom-call | tf_op jit(solution)/shard_map/jit(cholesky)/cholesky | solution.py:56
  802.9 8.8 %while.1 = (s32[]{:T(128)}, f32[512,512]{0,1:T(8,128)S(1)}, s32[4,2]{0,1:T(2,128)S(1)}, f32[4,128,128]{2,1,0:T(8,128)S(1)}, s32[]{:T(128)}) while((s32[]{:T(128)}, f32[512,512]{0,1:T(8,128)S(1)}, s32[4,2]{0,1:T(2,128)S(1)}, f32[4,128,128]{2,1,0:T(8,128)S(1)}, s32[]{:T(128)}) %tuple.30), condition=%wide.while_cond, body=%wide.while_body.sunk | while | flops 2 | bytes 393321 | solution.py:57
  803.6 1.4 dynamic-slice.7
  805.8 1.4 dynamic-slice.7
  808.0 1.4 dynamic-slice.7
  810.2 1.4 dynamic-slice.7
  811.7 39.3 %custom-call.37 = f32[4,128,128]{1,2,0:T(8,128)S(1)} custom-call(f32[4,128,128]{2,1,0:T(8,128)S(1)} %get-tuple-element.9), custom_call_target="InvertDiagBlocksLowerTriangular" | custom-call | tf_op jit(solution)/shard_map/jit(_solve_triangular)/triangular_solve | solution.py:57
  (92 shorter events, 21.2 us)
Async XLA Ops:
  7.2 328.5 %reduce-scatter.2.cloned.1.call-start = ((), (), s32[]{:S(2)}) async-start(), calls=%async_computation.2 | async-start | bytes 4325376 | tf_op jit(solution)/shard_map/reduce_scatter | solution.py:26
  234.7 337.6 %all-reduce.5.cloned.1.call-start = ((), (), s32[]{:S(2)}) async-start(), calls=%async_computation.3 | async-start | bytes 1048576 | tf_op jit(solution)/shard_map/psum | solution.py:46
  440.9 0.8 copy-start.2
  440.9 132.6 %copy-start.3 = (f32[512,128]{0,1:T(8,128)}, f32[512,128]{0,1:T(8,128)S(1)}, u32[]{:S(2)}) copy-start(f32[512,128]{0,1:T(8,128)S(1)} %get-tuple-element.28) | copy-start | bytes 786436
  441.7 273.5 %all-reduce.7.cloned.1.call-start = ((), (), s32[]{:S(2)}) async-start(), calls=%async_computation.4 | async-start | bytes 2621440 | tf_op jit(solution)/shard_map/psum | solution.py:55
  573.5 1.0 copy-start
  752.5 98.6 %copy-start.5 = (f32[512,128]{0,1:T(8,128)S(1)}, f32[512,128]{0,1:T(8,128)}, u32[]{:S(2)}) copy-start(f32[512,128]{0,1:T(8,128)} %get-tuple-element.25) | copy-start | bytes 786436
  763.1 90.3 %copy-start.1 = (f32[256,512]{0,1:T(8,128)S(1)}, f32[256,512]{0,1:T(8,128)}, u32[]{:S(2)}) copy-start(f32[256,512]{0,1:T(8,128)} %all-reduce.5.cloned.1.call-done) | copy-start | bytes 1572868
  802.9 53.0 %copy-start.4 = (f32[128,256]{1,0:T(8,128)S(1)}, f32[128,256]{1,0:T(8,128)}, u32[]{:S(2)}) copy-start(f32[128,256]{1,0:T(8,128)} %reduce-scatter.2.cloned.1.call-done) | copy-start | bytes 393220
Sparse Core Ops, SparseCore 0:
  234.8 100.8 reduce-scatter.1
  441.8 130.3 all-reduce.4
  574.7 140.5 all-reduce.6
